TPU v7x, 32 devices: a whole 2x2x4 slice. The times are simulated.
32 devices in a mesh: win: 4 (over y, core), pair: 8 (over z, x).
Axes of the slice: x: 2, y: 2, z: 4, core: 2. Of those that a mesh axis runs over, the one named last changes fastest.
Arguments:
- strain: bfloat16 [4, 2048, 7680], P('win', 'pair'), may hold values from -40 to 40
- pair_list: int32 [32, 2], replicated, may hold values from 0 to 15, as said below
- tile_live: int32 [32], P('pair'), may hold values 0 or 1
Outputs:
- stack: float32 [128, 32, 16, 128], P('win', 'pair')
Inputs may be any that keep to these rules, and one draw needn't show every extreme that they name: `pair_list`: rows q * 4 to (q + 1) * 4 - 1 are the tiles of owner q; the 8 block numbers in them fall into distinct groups of 2 consecutive blocks.
All inputs are finite; a program needn't handle non-finite values. No bound on the sum of `tile_live` on one device may be relied on, other than what follows from the above.
Results may differ from a plain program's by a relative error of at most 0.02.
Values may be sent and summed in bfloat16 or wider, within the bound.
No kernel may reach another device: no remote copies, remote signals or barrier semaphores. Data moves between devices by JAX's collectives and lax.ppermute only.
A program may use at most 64 MiB of HBM per device.

v0:
```python
import math
import jax
import jax.numpy as jnp
from jax import lax
from jax.sharding import PartitionSpec as P

C = 128
F = 384
LAGS = 16
DECIM = 32
B_DEV = 2


def dft_piece(first_row, row_count, sample_count, bin_count):
    sample_index = first_row + lax.iota(jnp.int32, row_count)
    bin_index = lax.iota(jnp.int32, bin_count) + 1
    product = sample_index[:, None] * bin_index[None, :] % sample_count
    angle = 2.0 * math.pi / sample_count * product.astype(jnp.float32)
    return jnp.concatenate([jnp.cos(angle), -jnp.sin(angle)], axis=1).astype(jnp.bfloat16)


def lag_tables(sample_count, bin_count, lag_count, stride):
    bin_index = lax.iota(jnp.int32, bin_count) + 1
    lag_shift = (lax.iota(jnp.int32, lag_count) - lag_count // 2) * stride
    product = bin_index[:, None] * lag_shift[None, :] % sample_count
    angle = 2.0 * math.pi / sample_count * product.astype(jnp.float32)
    return (jnp.cos(angle), jnp.sin(angle))


def whiten_rows(strain_rows, bin_count):
    row_total, sample_count = strain_rows.shape
    piece_len = sample_count // 4
    spectrum = jnp.zeros((row_total, 2 * bin_count), jnp.float32)
    for piece_index in range(4):
        dft_table = dft_piece(piece_index * piece_len, piece_len, sample_count, bin_count)
        samples_part = strain_rows[:, piece_index * piece_len : (piece_index + 1) * piece_len]
        spectrum = spectrum + jnp.dot(samples_part, dft_table, preferred_element_type=jnp.float32)
    real_part = spectrum[:, :bin_count]
    imag_part = spectrum[:, bin_count:]
    amplitude = jnp.sqrt(real_part * real_part + imag_part * imag_part)
    level = 0.2 * jnp.mean(amplitude, axis=1, keepdims=True) + 1e-06
    divisor = jnp.maximum(amplitude, level)
    return jnp.concatenate([real_part / divisor, imag_part / divisor], axis=1).astype(jnp.bfloat16)


def shift_block(spectrum_block, cos_lag, sin_lag):
    bin_count = cos_lag.shape[0]
    real_part = spectrum_block[:, :bin_count].astype(jnp.float32).T
    imag_part = spectrum_block[:, bin_count:].astype(jnp.float32).T
    upper_half = (
        real_part[:, None, :] * cos_lag[:, :, None] + imag_part[:, None, :] * sin_lag[:, :, None]
    )
    lower_half = (
        imag_part[:, None, :] * cos_lag[:, :, None] - real_part[:, None, :] * sin_lag[:, :, None]
    )
    joined = jnp.concatenate([upper_half, lower_half], axis=0).astype(jnp.bfloat16)
    return joined.reshape(2 * bin_count, -1)


def body(strain, pair_list, tile_live):
    window_count, local_rows, sample_count = strain.shape
    slot_count = tile_live.shape[0]
    pair_here = lax.axis_index("pair")
    flat_rows = strain.reshape(window_count * local_rows, sample_count)
    whitened = whiten_rows(flat_rows, F).reshape(window_count, B_DEV, C, 2 * F)
    local_blocks = jnp.transpose(whitened, (1, 0, 2, 3))
    wanted = lax.dynamic_slice_in_dim(pair_list, pair_here * slot_count, slot_count, 0).reshape(
        2 * slot_count
    )
    blank_slots = jnp.zeros((2 * slot_count,) + local_blocks.shape[1:], jnp.bfloat16)
    shard_rows = lax.all_gather(local_blocks, "pair", axis=0, tiled=True)
    block_count = shard_rows.shape[0]
    inside = (wanted >= 0) & (wanted < block_count)
    picked = jnp.take(shard_rows, jnp.clip(wanted, 0, block_count - 1), axis=0)
    needed = jnp.where(inside[:, None, None, None], picked, blank_slots)
    cos_lag, sin_lag = lag_tables(sample_count, F, LAGS, DECIM)
    own_rows = C // lax.axis_size("win")
    results = []
    for slot_index in range(slot_count):
        shifted = shift_block(needed[2 * slot_index + 1, 0], cos_lag, sin_lag)
        left_rows = needed[2 * slot_index, 0]
        summed = jnp.dot(left_rows, shifted, preferred_element_type=jnp.float32)
        results.append(summed)
    stacked = lax.psum_scatter(
        jnp.stack(results, axis=1).astype(jnp.bfloat16), "win", scatter_dimension=0, tiled=True
    ).astype(jnp.float32)
    live_local = tile_live.astype(jnp.float32)
    output = (
        stacked * live_local[None, :, None] / math.sqrt(F * window_count * lax.axis_size("win"))
    )
    return output.reshape(own_rows, slot_count, LAGS, C)


def solution(mesh):
    in_specs = (P("win", "pair", None), P(), P("pair"))
    out_specs = P("win", "pair", None, None)
    return jax.shard_map(body, mesh=mesh, in_specs=in_specs, out_specs=out_specs, check_vma=False)
```

profile of v0, /device:TPU:0, one launch (start us, length us, event | category | flops | bytes accessed | tf_op | source)
XLA Modules:
  0.0 182.1 jit_solution(2870586868444226078)
XLA Ops:
  6.6 50.0 %cosine_convert_fusion = (bf16[1920,384]{1,0:T(8,128)(2,1)S(1)}, bf16[1920,384]{1,0:T(8,128)(2,1)S(1)}, bf16[1920,384]{1,0:T(8,128)(2,1)S(1)}, bf16[1920,384]{1,...) fusion(s32[1920]{0:T(1024)S(1)} %get-tuple-element.47, ...), kind=kLoop, calls=%fused_computation.54 | loop fusion | flops 35389440 | bytes 11821056 | tf_op jit(solution)/shard_map/convert.36
  56.6 1.0 fusion.24
  57.6 1.0 fusion.86
  58.6 1.0 fusion.83
  59.6 1.0 fusion.80
  60.6 0.2 fusion.109
  60.8 0.2 divide_convert_fusion.1
  61.0 0.8 pad_maximum_fusion.1
  61.8 0.2 reduce-scatter.2.cloned.1.call-start
  62.1 0.1 dynamic-slice_clamp_fusion
  62.1 0.1 copy.43
  62.2 0.1 min.18
  62.3 0.1 min.16
  62.5 0.1 copy.42
  62.6 0.1 and.81
  62.7 0.2 fusion.98
  62.9 0.1 copy.48
  63.0 0.1 copy.50
  63.2 61.9 %all-gather.2.cloned.1.call-done = bf16[16,1,128,768]{3,2,1,0:T(8,128)(2,1)} async-done(((bf16[2,1,128,768]{3,2,1,0:T(8,128)(2,1)}), bf16[16,1,128,768]{3,2,1,0:T(8,128)(2,1)}) %all-gather.2.cloned.1.call-update) | async-done | bytes 3145744 | tf_op jit(solution)/shard_map/all_gather | solution.py:71
  125.1 2.5 %gather_fusion = bf16[8,128,768]{2,1,0:T(8,128)(2,1)S(1)} fusion(bf16[16,128,768]{2,1,0:T(8,128)(2,1)} %bitcast.116, s32[1024]{0:T(1024)S(1)} %pad_clamp_fusion), kind=kCustom, calls=%fused_computation | custom fusion | bytes 3145760 | tf_op jit(solution)/shard_map/jit(_take)/gather | solution.py:74
  127.7 0.2 fusion.76
  128.0 0.1 copy.47
  128.1 0.1 copy.49
  128.3 0.1 copy.51
  128.4 0.1 copy.52
  128.6 0.1 copy.53
  128.7 0.1 copy.54
  128.9 0.7 convert_bitcast_fusion.1
  129.6 0.1 copy.55
  129.7 1.1 copy.56
  130.8 4.3 %add_convert_fusion.3 = (bf16[384,16,128]{2,1,0:T(8,128)(2,1)S(1)}, bf16[384,16,128]{2,1,0:T(8,128)(2,1)S(1)}, bf16[384,16,128]{2,1,0:T(8,128)(2,1)S(1)}, bf16[3...) fusion(f32[384,16]{1,0:T(8,128)S(1)} %copy.50, ...), kind=kLoop, calls=%fused_computation.28 | loop fusion | flops 25165824 | bytes 14204928 | tf_op jit(solution)/shard_map/convert.31
  135.0 0.4 copy.81
  135.5 0.4 copy.82
  135.9 0.4 copy.79
  136.3 0.4 copy.80
  136.7 0.4 copy.77
  137.1 0.4 copy.78
  137.5 0.4 copy.75
  138.0 0.4 copy.76
  138.4 0.6 fusion.64
  139.0 0.6 fusion.67
  139.6 0.6 fusion.70
  140.2 0.6 fusion.73
  140.9 1.6 pad_maximum_fusion
  142.5 30.2 %reduce-scatter.2.cloned.1.call-done = bf16[32,4,2048]{2,0,1:T(8,128)(2,1)} async-done(((bf16[128,4,2048]{2,0,1:T(8,128)(2,1)}), bf16[32,4,2048]{2,0,1:T(8,128)(2,1)}) %reduce-scatter.2.cloned.1.call-update) | async-done | bytes 524304 | tf_op jit(solution)/shard_map/reduce_scatter | solution.py:84
  172.7 1.2 multiply_multiply_fusion
  174.0 0.2 copy.66
  174.1 1.1 copy.57
  (23 shorter events, 0.3 us)
Async XLA Ops:
  6.5 118.6 %all-gather.2.cloned.1.call-start = ((), (), s32[]{:S(2)}) async-start(), calls=%async_computation.1 | async-start | bytes 3538944 | tf_op jit(solution)/shard_map/all_gather | solution.py:71
  6.6 50.1 %copy-start.1 = (bf16[1,256,7680]{2,1,0:T(8,128)(2,1)S(1)}, bf16[1,256,7680]{2,1,0:T(8,128)(2,1)}, u32[]{:S(2)}) copy-start(bf16[1,256,7680]{2,1,0:T(8,128)(2,1)} %param.3) | copy-start | bytes 11796484
  60.6 1.5 copy-start
  61.8 110.9 %reduce-scatter.2.cloned.1.call-start = ((), (), s32[]{:S(2)}) async-start(), calls=%async_computation.2 | async-start | bytes 2621440 | tf_op jit(solution)/shard_map/reduce_scatter | solution.py:84
  140.9 1.6 copy-start.2
Sparse Core Ops, SparseCore 0:
  61.9 63.1 all-gather.1
  142.6 30.0 reduce-scatter.1
where the time goes:
time: 182 us
  waiting for transfers between devices  92.1 us (51%)
  other arithmetic  59.8 us (33%)
  between operations  13.8 us (8%)
  local copies, waits for them, and re-layouts  9.81 us (5%)
  matrix products  6.39 us (4%)
    all_gather x1, waiting for transfers between devices, body(): shard_rows = lax.all_gather(local_blocks, 'pair', axis=0, tiled=True)  61.9 us
    another operation x3, other arithmetic  54.5 us
    reduce_scatter x1, waiting for transfers between devices, body(): lax.psum_scatter(jnp.stack(results, axis=1).astype(jnp.bfloat16), 'win',...  30.2 us
    dot_general x4, matrix products, whiten_rows(): jnp.dot(samples_part, dft_table, preferred_element_type=jnp.float32)  3.91 us
  transfers between devices with their start and end apart: 2, of which 2 were waited for; matrix products, arithmetic and copies ran while one was open for 1% of the time, Pallas kernels for 0%

commit v1 on v0

--- a/solution.py
+++ b/solution.py
@@ -9,6 +9,22 @@
 LAGS = 16
 DECIM = 32
 B_DEV = 2
+
+
+def gather_around(x, axis, dim):
+    ways, here, step = (lax.axis_size(axis), lax.axis_index(axis), x.shape[dim])
+    shape = [n * ways if d == dim else n for d, n in enumerate(x.shape)]
+    full = lax.dynamic_update_slice_in_dim(jnp.zeros(shape, x.dtype), x, here * step, axis=dim)
+    going_up = going_down = x
+    for far in range(1, ways // 2 + 1):
+        going_up = lax.ppermute(going_up, axis, [(d, (d + 1) % ways) for d in range(ways)])
+        full = lax.dynamic_update_slice_in_dim(full, going_up, (here - far) % ways * step, axis=dim)
+        if 2 * far < ways:
+            going_down = lax.ppermute(going_down, axis, [(d, (d - 1) % ways) for d in range(ways)])
+            full = lax.dynamic_update_slice_in_dim(
+                full, going_down, (here + far) % ways * step, axis=dim
+            )
+    return full
 
 
 def dft_piece(first_row, row_count, sample_count, bin_count):
@@ -68,7 +84,7 @@
         2 * slot_count
     )
     blank_slots = jnp.zeros((2 * slot_count,) + local_blocks.shape[1:], jnp.bfloat16)
-    shard_rows = lax.all_gather(local_blocks, "pair", axis=0, tiled=True)
+    shard_rows = gather_around(local_blocks, "pair", 0)
     block_count = shard_rows.shape[0]
     inside = (wanted >= 0) & (wanted < block_count)
     picked = jnp.take(shard_rows, jnp.clip(wanted, 0, block_count - 1), axis=0)

time: 182 us -> 188 us (1.033)
  starting transfers between devices: 0.22 us -> 19.4 us
  waiting for transfers between devices: 92.1 us -> 74 us
  local copies, waits for them, and re-layouts: 9.81 us -> 13 us
    all_gather x1 -> x0, waiting for transfers between devices: 61.9 us -> none  [body(): shard_rows = lax.all_gather(local_blocks, 'pair', axis=0, tiled=True)]
    ppermute x0 -> x7, waiting for transfers between devices: none -> 43.9 us  [the longest x4 43.9 us: gather_around(): lax.ppermute(going_up, axis, [(d, (d + 1) % ways) for d in range(ways)])]
    ppermute x0 -> x7, starting transfers between devices: none -> 19.4 us  [the longest x4 10.3 us: gather_around(): lax.ppermute(going_up, axis, [(d, (d + 1) % ways) for d in range(ways)])]
    dynamic_update_slice x0 -> x8, local copies, waits for them, and re-layouts: none -> 2.51 us  [the longest x5 1.41 us: gather_around(): lax.dynamic_update_slice_in_dim(full, going_up, (here - far) % ways * ste...]
  transfers between devices with their start and end apart: 2 -> 8, of which waited for: 2 -> 5; matrix products, arithmetic and copies ran while one was open for 1% -> 3% of each run, Pallas kernels for 0% -> 0%
where the time goes in v1:
time: 188 us
  waiting for transfers between devices  74 us (39%)
  other arithmetic  61.3 us (33%)
  starting transfers between devices  19.4 us (10%)
  between operations  13.9 us (7%)
  local copies, waits for them, and re-layouts  13 us (7%)
  matrix products  6.4 us (3%)
    another operation x3, other arithmetic  54.5 us
    ppermute x4, waiting for transfers between devices, gather_around(): lax.ppermute(going_up, axis, [(d, (d + 1) % ways) for d in range(ways)])  43.9 us
    reduce_scatter x1, waiting for transfers between devices, body(): lax.psum_scatter(jnp.stack(results, axis=1).astype(jnp.bfloat16), 'win',...  30.1 us
    ppermute x4, starting transfers between devices, gather_around(): lax.ppermute(going_up, axis, [(d, (d + 1) % ways) for d in range(ways)])  10.3 us
    ppermute x3, starting transfers between devices, gather_around(): lax.ppermute(going_down, axis, [(d, (d - 1) % ways) for d in range(ways)])  9.12 us
    dot_general x4, matrix products, whiten_rows(): jnp.dot(samples_part, dft_table, preferred_element_type=jnp.float32)  3.91 us
  transfers between devices with their start and end apart: 8, of which 5 were waited for; matrix products, arithmetic and copies ran while one was open for 3% of the time, Pallas kernels for 0%

profile of v1, /device:TPU:0, one launch (start us, length us, event | category | flops | bytes accessed | tf_op | source)
XLA Modules:
  0.0 188.0 jit_solution(1688008071248173882)
XLA Ops:
  6.6 50.1 %cosine_convert_fusion = (bf16[1920,384]{1,0:T(8,128)(2,1)S(1)}, bf16[1920,384]{1,0:T(8,128)(2,1)S(1)}, bf16[1920,384]{1,0:T(8,128)(2,1)S(1)}, bf16[1920,384]{1,...) fusion(s32[1920]{0:T(1024)S(1)} %get-tuple-element.47, ...), kind=kLoop, calls=%fused_computation.54 | loop fusion | flops 35389440 | bytes 11821056 | tf_op jit(solution)/shard_map/convert.36
  56.7 1.0 fusion.24
  57.6 1.0 fusion.86
  58.6 1.0 fusion.83
  59.6 1.0 fusion.80
  60.6 0.2 fusion.110
  60.8 0.2 divide_convert_fusion.1
  61.1 0.8 pad_maximum_fusion.1
  61.8 2.9 %collective-permute-start = (bf16[2,1,128,768]{3,2,0,1:T(8,128)(2,1)}, bf16[2,1,128,768]{3,2,0,1:T(8,128)(2,1)}, u32[]{:S(2)}, u32[]{:S(2)}) collective-permute-start(bf16[2,1,128,768]{3,2,0,1:T(8,128)(2,1)} %pad_maximum_fusion.1), channel_id=1, source_target_pairs={{0,1},{1,2},{2,3},{3,4},{4,5},{5,6},{6,7},{7,0},{8,9},{9,10},{10,1... | collective-permute-start | bytes 1179656 | tf_op jit(solution)/shard_map/ppermute | solution.py:20
  64.8 3.0 %collective-permute-start.1 = (bf16[2,1,128,768]{3,2,0,1:T(8,128)(2,1)}, bf16[2,1,128,768]{3,2,0,1:T(8,128)(2,1)}, u32[]{:S(2)}, u32[]{:S(2)}) collective-permute-start(bf16[2,1,128,768]{3,2,0,1:T(8,128)(2,1)} %pad_maximum_fusion.1), channel_id=1, source_target_pairs={{0,7},{1,0},{2,1},{3,2},{4,3},{5,4},{6,5},{7,6},{8,15},{9,8},{10,9... | collective-permute-start | bytes 1179656 | tf_op jit(solution)/shard_map/ppermute | solution.py:23
  68.1 0.2 fusion.98
  68.7 0.8 copy.24
  69.5 0.8 copy.26
  70.4 0.3 broadcast.304
  70.7 11.2 %collective-permute-done = bf16[2,1,128,768]{3,2,0,1:T(8,128)(2,1)} collective-permute-done((bf16[2,1,128,768]{3,2,0,1:T(8,128)(2,1)}, bf16[2,1,128,768]{3,2,0,1:T(8,128)(2,1)}, u32[]{:S(2)}, u32[]{:S(2)}) %collective-permute-start) | collective-permute-done | bytes 393248 | tf_op jit(solution)/shard_map/ppermute | solution.py:20
  81.9 2.5 %collective-permute-start.2 = (bf16[2,1,128,768]{3,2,0,1:T(8,128)(2,1)}, bf16[2,1,128,768]{3,2,0,1:T(8,128)(2,1)S(1)}, u32[]{:S(2)}, u32[]{:S(2)}) collective-permute-start(bf16[2,1,128,768]{3,2,0,1:T(8,128)(2,1)} %collective-permute-done), channel_id=1, source_target_pairs={{0,1},{1,2},{2,3},{3,4},{4,5},{5,6},{6,7},{7,0},{8,9},{9,10},{10,1... | collective-permute-start | bytes 1179656 | tf_op jit(solution)/shard_map/ppermute | solution.py:20
  84.4 3.0 %collective-permute-start.3 = (bf16[2,1,128,768]{3,2,0,1:T(8,128)(2,1)}, bf16[2,1,128,768]{3,2,0,1:T(8,128)(2,1)S(1)}, u32[]{:S(2)}, u32[]{:S(2)}) collective-permute-start(bf16[2,1,128,768]{3,2,0,1:T(8,128)(2,1)} %collective-permute-done.1), channel_id=1, source_target_pairs={{0,7},{1,0},{2,1},{3,2},{4,3},{5,4},{6,5},{7,6},{8,15},{9,8},{10,9... | collective-permute-start | bytes 1179656 | tf_op jit(solution)/shard_map/ppermute | solution.py:23
  87.4 1.0 bitcast_dynamic-update-slice_fusion.6
  88.4 1.0 bitcast_dynamic-update-slice_fusion.5
  89.5 11.1 %collective-permute-done.2 = bf16[2,1,128,768]{3,2,0,1:T(8,128)(2,1)S(1)} collective-permute-done((bf16[2,1,128,768]{3,2,0,1:T(8,128)(2,1)}, bf16[2,1,128,768]{3,2,0,1:T(8,128)(2,1)S(1)}, u32[]{:S(2)}, u32[]{:S(2)}) %collective-permute-start.2) | collective-permute-done | bytes 393248 | tf_op jit(solution)/shard_map/ppermute | solution.py:20
  100.6 2.4 %collective-permute-start.4 = (bf16[2,1,128,768]{3,2,0,1:T(8,128)(2,1)S(1)}, bf16[2,1,128,768]{3,2,0,1:T(8,128)(2,1)S(1)}, u32[]{:S(2)}, u32[]{:S(2)}) collective-permute-start(bf16[2,1,128,768]{3,2,0,1:T(8,128)(2,1)S(1)} %collective-permute-done.2), channel_id=1, source_target_pairs={{0,1},{1,2},{2,3},{3,4},{4,5},{5,6},{6,7},{7,0},{8,9},{9,10},{10,1... | collective-permute-start | bytes 1179656 | tf_op jit(solution)/shard_map/ppermute | solution.py:20
  103.0 3.0 %collective-permute-start.5 = (bf16[2,1,128,768]{3,2,0,1:T(8,128)(2,1)S(1)}, bf16[2,1,128,768]{3,2,0,1:T(8,128)(2,1)S(1)}, u32[]{:S(2)}, u32[]{:S(2)}) collective-permute-start(bf16[2,1,128,768]{3,2,0,1:T(8,128)(2,1)S(1)} %collective-permute-done.3), channel_id=1, source_target_pairs={{0,7},{1,0},{2,1},{3,2},{4,3},{5,4},{6,5},{7,6},{8,15},{9,8},{10,9... | collective-permute-start | bytes 1179656 | tf_op jit(solution)/shard_map/ppermute | solution.py:23
  106.1 12.0 %collective-permute-done.4 = bf16[2,1,128,768]{3,2,0,1:T(8,128)(2,1)S(1)} collective-permute-done((bf16[2,1,128,768]{3,2,0,1:T(8,128)(2,1)S(1)}, bf16[2,1,128,768]{3,2,0,1:T(8,128)(2,1)S(1)}, u32[]{:S(2)}, u32[]{:S(2)}) %collective-permute-start.4) | collective-permute-done | bytes 393248 | tf_op jit(solution)/shard_map/ppermute | solution.py:20
  118.1 2.5 %collective-permute-start.6 = (bf16[2,1,128,768]{3,2,0,1:T(8,128)(2,1)S(1)}, bf16[2,1,128,768]{3,2,0,1:T(8,128)(2,1)S(1)}, u32[]{:S(2)}, u32[]{:S(2)}) collective-permute-start(bf16[2,1,128,768]{3,2,0,1:T(8,128)(2,1)S(1)} %collective-permute-done.4), channel_id=1, source_target_pairs={{0,1},{1,2},{2,3},{3,4},{4,5},{5,6},{6,7},{7,0},{8,9},{9,10},{10,1... | collective-permute-start | bytes 1179656 | tf_op jit(solution)/shard_map/ppermute | solution.py:20
  120.7 9.6 %collective-permute-done.6 = bf16[2,1,128,768]{3,2,0,1:T(8,128)(2,1)S(1)} collective-permute-done((bf16[2,1,128,768]{3,2,0,1:T(8,128)(2,1)S(1)}, bf16[2,1,128,768]{3,2,0,1:T(8,128)(2,1)S(1)}, u32[]{:S(2)}, u32[]{:S(2)}) %collective-permute-start.6) | collective-permute-done | bytes 393248 | tf_op jit(solution)/shard_map/ppermute | solution.py:20
  130.3 1.8 gather_fusion
  132.1 1.6 fusion.76
  134.0 0.1 copy.25
  134.8 0.7 convert_bitcast_fusion.1
  135.6 1.1 copy.32
  136.7 4.3 %add_convert_fusion.3 = (bf16[384,16,128]{2,1,0:T(8,128)(2,1)S(1)}, bf16[384,16,128]{2,1,0:T(8,128)(2,1)S(1)}, bf16[384,16,128]{2,1,0:T(8,128)(2,1)S(1)}, bf16[3...) fusion(f32[384,16]{1,0:T(8,128)S(1)} %copy-done.1, ...), kind=kLoop, calls=%fused_computation.28 | loop fusion | flops 25165824 | bytes 14204928 | tf_op jit(solution)/shard_map/convert.31
  140.9 0.4 copy.57
  141.4 0.4 copy.58
  141.8 0.4 copy.55
  142.2 0.4 copy.56
  142.6 0.4 copy.53
  143.0 0.4 copy.54
  143.4 0.4 copy.51
  143.9 0.4 copy.52
  144.3 0.6 fusion.64
  144.9 0.6 fusion.67
  145.5 0.6 fusion.70
  146.2 0.6 fusion.73
  146.8 1.6 pad_maximum_fusion
  148.5 30.1 %reduce-scatter.2.cloned.1.call-done = bf16[32,4,2048]{2,0,1:T(8,128)(2,1)} async-done(((bf16[128,4,2048]{2,0,1:T(8,128)(2,1)}), bf16[32,4,2048]{2,0,1:T(8,128)(2,1)}) %reduce-scatter.2.cloned.1.call-update) | async-done | bytes 524304 | tf_op jit(solution)/shard_map/reduce_scatter | solution.py:100
  178.6 1.2 multiply_multiply_fusion
  179.8 0.2 copy.42
  180.0 1.1 copy.33
  (47 shorter events, 1.8 us)
Async XLA Ops:
  6.5 172.0 %reduce-scatter.2.cloned.1.call-start = ((), (), s32[]{:S(2)}) async-start(), calls=%async_computation.1 | async-start | bytes 2621440 | tf_op jit(solution)/shard_map/reduce_scatter | solution.py:100
  6.6 50.1 %copy-start.3 = (bf16[1,256,7680]{2,1,0:T(8,128)(2,1)S(1)}, bf16[1,256,7680]{2,1,0:T(8,128)(2,1)}, u32[]{:S(2)}) copy-start(bf16[1,256,7680]{2,1,0:T(8,128)(2,1)} %param.3) | copy-start | bytes 11796484
  59.6 8.2 %copy-start.2 = (s32[32,2]{0,1:T(2,128)S(1)}, s32[32,2]{0,1:T(2,128)}, u32[]{:S(2)}) copy-start(s32[32,2]{0,1:T(2,128)} %param.4) | copy-start | bytes 772
  61.8 20.1 %collective-permute-start = (bf16[2,1,128,768]{3,2,0,1:T(8,128)(2,1)}, bf16[2,1,128,768]{3,2,0,1:T(8,128)(2,1)}, u32[]{:S(2)}, u32[]{:S(2)}) collective-permute-start(bf16[2,1,128,768]{3,2,0,1:T(8,128)(2,1)} %pad_maximum_fusion.1), channel_id=1, source_target_pairs={{0,1},{1,2},{2,3},{3,4},{4,5},{5,6},{6,7},{7,0},{8,9},{9,10},{10,1... | collective-permute-start | bytes 1179656 | tf_op jit(solution)/shard_map/ppermute | solution.py:20
  64.8 19.6 %collective-permute-start.1 = (bf16[2,1,128,768]{3,2,0,1:T(8,128)(2,1)}, bf16[2,1,128,768]{3,2,0,1:T(8,128)(2,1)}, u32[]{:S(2)}, u32[]{:S(2)}) collective-permute-start(bf16[2,1,128,768]{3,2,0,1:T(8,128)(2,1)} %pad_maximum_fusion.1), channel_id=1, source_target_pairs={{0,7},{1,0},{2,1},{3,2},{4,3},{5,4},{6,5},{7,6},{8,15},{9,8},{10,9... | collective-permute-start | bytes 1179656 | tf_op jit(solution)/shard_map/ppermute | solution.py:23
  81.9 18.7 %collective-permute-start.2 = (bf16[2,1,128,768]{3,2,0,1:T(8,128)(2,1)}, bf16[2,1,128,768]{3,2,0,1:T(8,128)(2,1)S(1)}, u32[]{:S(2)}, u32[]{:S(2)}) collective-permute-start(bf16[2,1,128,768]{3,2,0,1:T(8,128)(2,1)} %collective-permute-done), channel_id=1, source_target_pairs={{0,1},{1,2},{2,3},{3,4},{4,5},{5,6},{6,7},{7,0},{8,9},{9,10},{10,1... | collective-permute-start | bytes 1179656 | tf_op jit(solution)/shard_map/ppermute | solution.py:20
  84.4 18.6 %collective-permute-start.3 = (bf16[2,1,128,768]{3,2,0,1:T(8,128)(2,1)}, bf16[2,1,128,768]{3,2,0,1:T(8,128)(2,1)S(1)}, u32[]{:S(2)}, u32[]{:S(2)}) collective-permute-start(bf16[2,1,128,768]{3,2,0,1:T(8,128)(2,1)} %collective-permute-done.1), channel_id=1, source_target_pairs={{0,7},{1,0},{2,1},{3,2},{4,3},{5,4},{6,5},{7,6},{8,15},{9,8},{10,9... | collective-permute-start | bytes 1179656 | tf_op jit(solution)/shard_map/ppermute | solution.py:23
  100.6 17.5 %collective-permute-start.4 = (bf16[2,1,128,768]{3,2,0,1:T(8,128)(2,1)S(1)}, bf16[2,1,128,768]{3,2,0,1:T(8,128)(2,1)S(1)}, u32[]{:S(2)}, u32[]{:S(2)}) collective-permute-start(bf16[2,1,128,768]{3,2,0,1:T(8,128)(2,1)S(1)} %collective-permute-done.2), channel_id=1, source_target_pairs={{0,1},{1,2},{2,3},{3,4},{4,5},{5,6},{6,7},{7,0},{8,9},{9,10},{10,1... | collective-permute-start | bytes 1179656 | tf_op jit(solution)/shard_map/ppermute | solution.py:20
  103.0 17.7 %collective-permute-start.5 = (bf16[2,1,128,768]{3,2,0,1:T(8,128)(2,1)S(1)}, bf16[2,1,128,768]{3,2,0,1:T(8,128)(2,1)S(1)}, u32[]{:S(2)}, u32[]{:S(2)}) collective-permute-start(bf16[2,1,128,768]{3,2,0,1:T(8,128)(2,1)S(1)} %collective-permute-done.3), channel_id=1, source_target_pairs={{0,7},{1,0},{2,1},{3,2},{4,3},{5,4},{6,5},{7,6},{8,15},{9,8},{10,9... | collective-permute-start | bytes 1179656 | tf_op jit(solution)/shard_map/ppermute | solution.py:23
  118.1 12.1 %collective-permute-start.6 = (bf16[2,1,128,768]{3,2,0,1:T(8,128)(2,1)S(1)}, bf16[2,1,128,768]{3,2,0,1:T(8,128)(2,1)S(1)}, u32[]{:S(2)}, u32[]{:S(2)}) collective-permute-start(bf16[2,1,128,768]{3,2,0,1:T(8,128)(2,1)S(1)} %collective-permute-done.4), channel_id=1, source_target_pairs={{0,1},{1,2},{2,3},{3,4},{4,5},{5,6},{6,7},{7,0},{8,9},{9,10},{10,1... | collective-permute-start | bytes 1179656 | tf_op jit(solution)/shard_map/ppermute | solution.py:20
  133.8 2.8 %copy-start = (f32[384,16]{1,0:T(8,128)S(1)}, f32[384,16]{1,0:T(8,128)}, u32[]{:S(2)}) copy-start(f32[384,16]{1,0:T(8,128)} %copy.24) | copy-start | bytes 73732
  133.8 2.8 %copy-start.1 = (f32[384,16]{1,0:T(8,128)S(1)}, f32[384,16]{1,0:T(8,128)}, u32[]{:S(2)}) copy-start(f32[384,16]{1,0:T(8,128)} %copy.26) | copy-start | bytes 73732
  146.8 1.6 copy-start.4
Sparse Core Ops, SparseCore 0:
  148.6 29.9 reduce-scatter.1
